TPU v7x, 128 devices: a whole 4x4x4 slice. The times are simulated.
128 devices in a mesh: aux: 4 (over x), row: 32 (over z, y, core).
Axes of the slice: x: 4, y: 4, z: 4, core: 2. Of those that a mesh axis runs over, the one named last changes fastest.
Arguments:
- b_tiles: bfloat16 [4, 32768, 2048], P('aux', 'row'), may hold values from -0.125 to 0.125
- occ_coeff: bfloat16 [32768, 256], P('row'), may hold values from -3 to 3
- tile_blocks: int32 [256, 16], P('row'), may hold values from 0 to 255, as said below
- screen_mask: int32 [256, 16], P('row'), may hold values from 0 to 1, as said below
Outputs:
- exchange: bfloat16 [32768, 32, 4, 256], P('row', None, 'aux')
Inputs may be any that keep to these rules, and one draw needn't show every extreme that they name: `tile_blocks`: each entry names a basis block at most 8 blocks away from its own row's block; the first slot of every block names the block itself. `screen_mask`: in every basis block the kept slots come first; some block keeps all 16.
All inputs are finite; a program needn't handle non-finite values.
Results may differ from a plain program's by a relative error of at most 0.0057.
Values may be sent and summed in bfloat16 or wider, within the bound.
No kernel may reach another device: no remote copies, remote signals or barrier semaphores. Data moves between devices by JAX's collectives and lax.ppermute only.
A program may use at most 128 MiB of HBM per device.

v0:
```python
import jax
import jax.numpy as jnp
from jax import lax
from jax.sharding import Mesh, PartitionSpec as P


def with_halo(block, sides, width):
    for axis, dim in sides:
        count = lax.axis_size(axis)
        forward = [(i, i + 1) for i in range(count - 1)]
        backward = [(target, source) for source, target in forward]
        low = lax.ppermute(
            lax.slice_in_dim(block, block.shape[dim] - width, None, axis=dim), axis, forward
        )
        high = lax.ppermute(lax.slice_in_dim(block, 0, width, axis=dim), axis, backward)
        block = jnp.concatenate([low, block, high], axis=dim)
    return block


ROW = ("rzy", "core")


def per_device(b_tiles, occ_coeff, tile_blocks, screen_mask):
    p_local, rows_local, stored = b_tiles.shape
    blocks_local, slot_count = tile_blocks.shape
    block_size = rows_local // blocks_local
    orbitals = occ_coeff.shape[1]
    aux_count = lax.axis_size("aux")
    row_index = lax.axis_index(ROW)
    extended = with_halo(occ_coeff, ((ROW, 0),), rows_local)
    coeff_blocks = extended.reshape(3 * blocks_local, block_size, orbitals)
    local_index = tile_blocks - (row_index - 1) * blocks_local
    picked = jnp.take(coeff_blocks, local_index, axis=0)
    keep_mask = screen_mask.astype(jnp.bfloat16)
    tiles_five = b_tiles.reshape(p_local, blocks_local, block_size, slot_count, block_size)
    masked = picked * keep_mask[:, :, None, None]
    half_sum = jnp.einsum(
        "pbmsn,bsni->pbmi", tiles_five, masked, preferred_element_type=jnp.float32
    )
    half_local = half_sum.astype(jnp.bfloat16).reshape(p_local, rows_local, orbitals)
    slab_rows = lax.all_gather(half_local, "aux", axis=0, tiled=True)
    share = rows_local // aux_count
    piece = lax.dynamic_slice_in_dim(slab_rows, lax.axis_index("aux") * share, share, axis=1)
    plane = lax.all_gather(piece, "rzy", axis=0)
    partner = lax.all_gather(plane, "core", axis=1)
    chips, cores = partner.shape[:2]
    partner = partner.reshape(chips * cores, *piece.shape)
    result = jnp.einsum("pmi,rpki->mrk", slab_rows, partner, preferred_element_type=jnp.float32)
    return result.astype(jnp.bfloat16).reshape(rows_local, chips * cores, 1, share)


def solution(mesh):
    aux_count, row_count = mesh.devices.shape
    devices = mesh.devices.reshape(aux_count, row_count // 2, 2)
    split_mesh = Mesh(devices, ("aux",) + ROW)
    in_specs = (P("aux", ROW, None), P(ROW, None), P(ROW, None), P(ROW, None))
    out_specs = P(ROW, None, "aux", None)
    return jax.shard_map(
        per_device, mesh=split_mesh, in_specs=in_specs, out_specs=out_specs, check_vma=False
    )
```

profile of v0, /device:TPU:1, one launch (start us, length us, event | category | flops | bytes accessed | tf_op | source)
XLA Modules:
  0.0 227.2 jit_solution(13417141563487165089)
XLA Ops:
  6.5 0.0 copy-start
  6.5 0.0 all-gather.6.cloned.1.call-start
  6.5 4.7 %collective-permute-start = (bf16[1024,256]{1,0:T(8,128)(2,1)}, bf16[1024,256]{1,0:T(8,128)(2,1)S(1)}, u32[]{:S(2)}, u32[]{:S(2)}) collective-permute-start(bf16[1024,256]{1,0:T(8,128)(2,1)} %param.5), channel_id=1, source_target_pairs={{0,1},{1,2},{2,3},{3,4},{4,5},{5,6},{6,7},{7,8},{8,9},{9,10},{10,1... | collective-permute-start | bytes 1572872 | tf_op jit(solution)/shard_map/ppermute | solution.py:12
  11.3 1.9 collective-permute-start.1
  13.2 0.7 convert_element_type.15
  13.9 0.7 compare_and_fusion
  14.6 0.1 reshape.32
  14.7 5.6 %copy.11 = bf16[128,8,16,128]{3,2,1,0:T(8,128)(2,1)} copy(bf16[128,8,16,128]{3,1,2,0:T(8,128)(2,1)} %bitcast.32) | data formatting | bytes 8388608
  20.2 0.0 collective-permute-done
  20.2 1.7 collective-permute-done.1
  22.0 0.0 copy-done
  22.0 0.1 pad_maximum_fusion
  22.1 6.7 %gather_fusion = bf16[128,128,256]{2,1,0:T(8,128)(2,1)} fusion(bf16[24,128,256]{2,1,0:T(8,128)(2,1)S(1)} %bitcast.29, s32[1024]{0:T(1024)S(1)} %pad_clamp_fusion), kind=kCustom, calls=%fused_computation | custom fusion | bytes 16777728 | tf_op jit(solution)/shard_map/jit(_take)/gather | solution.py:33
  28.8 8.1 %fusion.14 = bf16[8,256,128]{1,2,0:T(8,128)(2,1)} fusion(bf16[8,16,128,256]{3,2,1,0:T(8,128)(2,1)} %bitcast.30, pred[8,16]{1,0:T(8,128)(4,1)S(1)} %get-tuple-element.5, bf16[8,16]{1,0:T(8,128)(2,1)S(1)} %convert_element_type.15, bf16[8,128,16,128]{3,2,1,0:T(8,128)(2,1)} %bitcast.33), kind=kOutput, calls=%fused_computation.13 | convolution fusion | flops 1094975488 | bytes 13107584 | tf_op jit(solution)/shard_map/pbmsn,bsni->pbmi/dot_general | solution.py:37
  37.0 0.0 all-gather.6.cloned.1.call-update
  37.0 0.0 all-gather.8.cloned.1.call-start
  37.0 34.2 %all-gather.6.cloned.1.call-done = bf16[4,1024,256]{2,1,0:T(8,128)(2,1)} async-done(((bf16[1,1024,256]{2,1,0:T(8,128)(2,1)}), bf16[4,1024,256]{2,1,0:T(8,128)(2,1)}) %all-gather.6.cloned.1.call-update) | async-done | bytes 2097168 | tf_op jit(solution)/shard_map/all_gather | solution.py:41
  71.3 0.0 copy-start.1
  71.3 2.0 constant_dynamic-slice_fusion
  73.3 0.0 all-gather.8.cloned.1.call-update
  73.3 0.0 all-gather.10.cloned.1.call-start
  73.4 71.0 %all-gather.8.cloned.1.call-done = bf16[64,256,256]{2,1,0:T(8,128)(2,1)} async-done(((bf16[4,256,256]{2,1,0:T(8,128)(2,1)}), bf16[64,256,256]{2,1,0:T(8,128)(2,1)}) %all-gather.8.cloned.1.call-update) | async-done | bytes 8388624 | tf_op jit(solution)/shard_map/all_gather | solution.py:44
  144.4 0.0 all-gather.10.cloned.1.call-update
  144.4 34.5 %all-gather.10.cloned.1.call-done = bf16[16,8,256,256]{3,2,1,0:T(8,128)(2,1)} async-done(((bf16[16,4,256,256]{3,2,1,0:T(8,128)(2,1)}), bf16[16,8,256,256]{3,2,1,0:T(8,128)(2,1)}) %all-gather.10.cloned.1.call-update) | async-done | bytes 16777232 | tf_op jit(solution)/shard_map/all_gather | solution.py:45
  178.9 0.0 copy-done.1
  178.9 23.9 %fusion = bf16[1024,32,1,256]{3,0,1,2:T(8,128)(2,1)} fusion(bf16[32,4,256,256]{3,2,1,0:T(8,128)(2,1)} %bitcast.35, bf16[4,1024,256]{2,1,0:T(8,128)(2,1)S(1)} %copy-done.1), kind=kOutput, calls=%fused_computation.2 | convolution fusion | flops 17188257792 | bytes 35651584 | tf_op jit(solution)/shard_map/pmi,rpki->mrk/dot_general | solution.py:48
  202.8 17.9 %copy.8 = bf16[1024,32,1,256]{3,1,2,0:T(8,128)(2,1)} copy(bf16[1024,32,1,256]{3,0,1,2:T(8,128)(2,1)} %fusion) | data formatting | bytes 33554432 | tf_op jit(solution)/shard_map/reshape | solution.py:49
  (1 shorter events, 0.0 us)
Async XLA Ops:
  6.5 15.4 %copy-start = (bf16[1024,256]{1,0:T(8,128)(2,1)S(1)}, bf16[1024,256]{1,0:T(8,128)(2,1)}, u32[]{:S(2)}) copy-start(bf16[1024,256]{1,0:T(8,128)(2,1)} %param.5) | copy-start | bytes 1572868
  6.5 64.7 %all-gather.6.cloned.1.call-start = ((), (), s32[]{:S(2)}) async-start(), calls=%async_computation | async-start | bytes 2621440 | tf_op jit(solution)/shard_map/all_gather | solution.py:41
  6.5 13.7 %collective-permute-start = (bf16[1024,256]{1,0:T(8,128)(2,1)}, bf16[1024,256]{1,0:T(8,128)(2,1)S(1)}, u32[]{:S(2)}, u32[]{:S(2)}) collective-permute-start(bf16[1024,256]{1,0:T(8,128)(2,1)} %param.5), channel_id=1, source_target_pairs={{0,1},{1,2},{2,3},{3,4},{4,5},{5,6},{6,7},{7,8},{8,9},{9,10},{10,1... | collective-permute-start | bytes 1572872 | tf_op jit(solution)/shard_map/ppermute | solution.py:12
  11.3 10.7 %collective-permute-start.1 = (bf16[1024,256]{1,0:T(8,128)(2,1)}, bf16[1024,256]{1,0:T(8,128)(2,1)S(1)}, u32[]{:S(2)}, u32[]{:S(2)}) collective-permute-start(bf16[1024,256]{1,0:T(8,128)(2,1)} %param.5), channel_id=1, source_target_pairs={{1,0},{2,1},{3,2},{4,3},{5,4},{6,5},{7,6},{8,7},{9,8},{10,9},{11,1... | collective-permute-start | bytes 1572872 | tf_op jit(solution)/shard_map/ppermute | solution.py:15
  37.0 107.4 %all-gather.8.cloned.1.call-start = ((), (), s32[]{:S(2)}) async-start(), calls=%async_computation.1 | async-start | bytes 8912896 | tf_op jit(solution)/shard_map/all_gather | solution.py:44
  71.3 107.6 %copy-start.1 = (bf16[4,1024,256]{2,1,0:T(8,128)(2,1)S(1)}, bf16[4,1024,256]{2,1,0:T(8,128)(2,1)}, u32[]{:S(2)}) copy-start(bf16[4,1024,256]{2,1,0:T(8,128)(2,1)} %all-gather.6.cloned.1.call-done) | copy-start | bytes 6291460
  73.3 105.6 %all-gather.10.cloned.1.call-start = ((), (), s32[]{:S(2)}) async-start(), calls=%async_computation.2 | async-start | bytes 25165824 | tf_op jit(solution)/shard_map/all_gather | solution.py:45
Sparse Core Ops, SparseCore 0:
  37.1 34.1 all-gather.5
  73.4 70.8 all-gather.7
  146.1 32.7 all-gather.9
where the time goes:
time: 228 us; the launch traced here: 227 us
  waiting for transfers between devices  142 us (62%)
  local copies, waits for them, and re-layouts  32.3 us (14%)
  matrix products  32 us (14%)
  between operations  13.1 us (6%)
  starting transfers between devices  6.72 us (3%)
    all_gather x1, waiting for transfers between devices, per_device(): plane = lax.all_gather(piece, 'rzy', axis=0)  71 us
    all_gather x1, waiting for transfers between devices, per_device(): partner = lax.all_gather(plane, 'core', axis=1)  34.5 us
    all_gather x1, waiting for transfers between devices, per_device(): slab_rows = lax.all_gather(half_local, 'aux', axis=0, tiled=True)  34.2 us
    dot_general x1, matrix products, per_device(): jnp.einsum('pmi,rpki->mrk', slab_rows, partner, preferred_element_type=jn...  23.9 us
    reshape x1, local copies, waits for them, and re-layouts, per_device(): result.astype(jnp.bfloat16).reshape(rows_local, chips * cores, 1, share)  17.9 us
    dot_general x1, matrix products, per_device(): jnp.einsum('pbmsn,bsni->pbmi', tiles_five, masked, preferred_element_type...  8.14 us
    gather x1, local copies, waits for them, and re-layouts, per_device(): picked = jnp.take(coeff_blocks, local_index, axis=0)  6.75 us
    unnamed x5, local copies, waits for them, and re-layouts  5.56 us
  transfers between devices with their start and end apart: 5, of which 4 were waited for; matrix products, arithmetic and copies ran while one was open for 3% of the time, Pallas kernels for 0%

commit v1 on v0

--- a/solution.py
+++ b/solution.py
@@ -38,7 +38,12 @@
         "pbmsn,bsni->pbmi", tiles_five, masked, preferred_element_type=jnp.float32
     )
     half_local = half_sum.astype(jnp.bfloat16).reshape(p_local, rows_local, orbitals)
-    slab_rows = lax.all_gather(half_local, "aux", axis=0, tiled=True)
+    ring = [half_local]
+    for hop in range(3):
+        ring.append(lax.ppermute(ring[-1], "aux", [(dev, (dev + 1) % 4) for dev in range(4)]))
+    slab_rows = jnp.roll(
+        jnp.concatenate(ring[::-1], axis=0), (lax.axis_index("aux") + 1) * ring[0].shape[0], axis=0
+    )
     share = rows_local // aux_count
     piece = lax.dynamic_slice_in_dim(slab_rows, lax.axis_index("aux") * share, share, axis=1)
     plane = lax.all_gather(piece, "rzy", axis=0)

time: 228 us -> 238 us (1.044)
  waiting for transfers between devices: 142 us -> 149 us
    ppermute x0 -> x3, waiting for transfers between devices: none -> 35.2 us  [per_device(): lax.ppermute(ring[-1], 'aux', [(dev, (dev + 1) % 4) for dev in range(4)])]
    all_gather x1 -> x0, waiting for transfers between devices: 34.2 us -> none  [per_device(): slab_rows = lax.all_gather(half_local, 'aux', axis=0, tiled=True)]
    all_gather x1, waiting for transfers between devices: 71 us -> 77.3 us  [per_device(): plane = lax.all_gather(piece, 'rzy', axis=0)]
    unnamed x5 -> x12, local copies, waits for them, and re-layouts: 5.56 us -> 7.88 us
  transfers between devices with their start and end apart: 5 -> 7, of which waited for: 4 -> 6; matrix products, arithmetic and copies ran while one was open for 3% -> 3% of each run, Pallas kernels for 0% -> 0%
where the time goes in v1:
time: 238 us; the launch traced here: 237 us
  waiting for transfers between devices  149 us (63%)
  local copies, waits for them, and re-layouts  33.5 us (14%)
  matrix products  31.4 us (13%)
  between operations  13.5 us (6%)
  starting transfers between devices  8.49 us (4%)
    all_gather x1, waiting for transfers between devices, per_device(): plane = lax.all_gather(piece, 'rzy', axis=0)  77.3 us
    ppermute x3, waiting for transfers between devices, per_device(): lax.ppermute(ring[-1], 'aux', [(dev, (dev + 1) % 4) for dev in range(4)])  35.2 us
    all_gather x1, waiting for transfers between devices, per_device(): partner = lax.all_gather(plane, 'core', axis=1)  34.5 us
    dot_general x1, matrix products, per_device(): jnp.einsum('pmi,rpki->mrk', slab_rows, partner, preferred_element_type=jn...  24.1 us
    reshape x1, local copies, waits for them, and re-layouts, per_device(): result.astype(jnp.bfloat16).reshape(rows_local, chips * cores, 1, share)  17.9 us
    unnamed x12, local copies, waits for them, and re-layouts  7.88 us
    dot_general x1, matrix products, per_device(): jnp.einsum('pbmsn,bsni->pbmi', tiles_five, masked, preferred_element_type...  7.35 us
    gather x1, local copies, waits for them, and re-layouts, per_device(): picked = jnp.take(coeff_blocks, local_index, axis=0)  6.75 us
  transfers between devices with their start and end apart: 7, of which 6 were waited for; matrix products, arithmetic and copies ran while one was open for 3% of the time, Pallas kernels for 0%

profile of v1, /device:TPU:1, one launch (start us, length us, event | category | flops | bytes accessed | tf_op | source)
XLA Modules:
  0.0 237.1 jit_solution(4242100654041030093)
XLA Ops:
  6.5 0.0 all-gather.5.cloned.1.call-start
  6.5 4.6 %collective-permute-start = (bf16[1024,256]{1,0:T(8,128)(2,1)}, bf16[1024,256]{1,0:T(8,128)(2,1)S(1)}, u32[]{:S(2)}, u32[]{:S(2)}) collective-permute-start(bf16[1024,256]{1,0:T(8,128)(2,1)} %param.5), channel_id=1, source_target_pairs={{0,1},{1,2},{2,3},{3,4},{4,5},{5,6},{6,7},{7,8},{8,9},{9,10},{10,1... | collective-permute-start | bytes 1572872 | tf_op jit(solution)/shard_map/ppermute | solution.py:12
  11.1 1.9 collective-permute-start.1
  13.1 0.7 convert_element_type.15
  13.8 0.7 compare_and_fusion
  14.5 0.1 reshape.32
  14.5 0.0 copy-start
  14.5 5.6 %copy.11 = bf16[128,8,16,128]{3,2,1,0:T(8,128)(2,1)} copy(bf16[128,8,16,128]{3,1,2,0:T(8,128)(2,1)} %bitcast.32) | data formatting | bytes 8388608
  20.2 0.0 collective-permute-done
  20.2 1.7 collective-permute-done.1
  21.8 0.0 copy-done
  21.8 0.1 pad_maximum_fusion
  22.0 6.7 %gather_fusion = bf16[128,128,256]{2,1,0:T(8,128)(2,1)} fusion(bf16[24,128,256]{2,1,0:T(8,128)(2,1)S(1)} %bitcast.29, s32[1024]{0:T(1024)S(1)} %pad_clamp_fusion), kind=kCustom, calls=%fused_computation | custom fusion | bytes 16777728 | tf_op jit(solution)/shard_map/jit(_take)/gather | solution.py:33
  28.7 7.3 %fusion.15 = bf16[8,256,128]{1,2,0:T(8,128)(2,1)S(1)} fusion(bf16[8,16,128,256]{3,2,1,0:T(8,128)(2,1)} %bitcast.30, pred[8,16]{1,0:T(8,128)(4,1)S(1)} %get-tuple-element.5, bf16[8,16]{1,0:T(8,128)(2,1)S(1)} %convert_element_type.15, bf16[8,128,16,128]{3,2,1,0:T(8,128)(2,1)} %bitcast.33), kind=kOutput, calls=%fused_computation.14 | convolution fusion | flops 1094975488 | bytes 13107584 | tf_op jit(solution)/shard_map/pbmsn,bsni->pbmi/dot_general | solution.py:37
  36.1 1.3 collective-permute-start.2
  37.3 10.0 %collective-permute-done.2 = bf16[1,1024,256]{2,1,0:T(8,128)(2,1)S(1)} collective-permute-done((bf16[1,1024,256]{2,1,0:T(8,128)(2,1)S(1)}, bf16[1,1024,256]{2,1,0:T(8,128)(2,1)S(1)}, u32[]{:S(2)}, u32[]{:S(2)}) %collective-permute-start.2) | collective-permute-done | bytes 524320 | tf_op jit(solution)/shard_map/ppermute | solution.py:43
  47.3 0.5 collective-permute-start.3
  47.8 11.8 %collective-permute-done.3 = bf16[1,1024,256]{2,1,0:T(8,128)(2,1)S(1)} collective-permute-done((bf16[1,1024,256]{2,1,0:T(8,128)(2,1)S(1)}, bf16[1,1024,256]{2,1,0:T(8,128)(2,1)S(1)}, u32[]{:S(2)}, u32[]{:S(2)}) %collective-permute-start.3) | collective-permute-done | bytes 524320 | tf_op jit(solution)/shard_map/ppermute | solution.py:43
  59.6 0.0 collective-permute-start.4
  59.6 13.4 %collective-permute-done.4 = bf16[1,1024,256]{2,1,0:T(8,128)(2,1)S(1)} collective-permute-done((bf16[1,1024,256]{2,1,0:T(8,128)(2,1)S(1)}, bf16[1,1024,256]{2,1,0:T(8,128)(2,1)S(1)}, u32[]{:S(2)}, u32[]{:S(2)}) %collective-permute-start.4) | collective-permute-done | bytes 524320 | tf_op jit(solution)/shard_map/ppermute | solution.py:43
  73.4 0.0 copy-start.1
  73.4 2.0 copy-done.1
  75.4 0.9 constant_dynamic-slice_fusion
  76.3 0.0 all-gather.5.cloned.1.call-update
  76.3 0.2 all-gather.7.cloned.1.call-start
  76.6 77.3 %all-gather.5.cloned.1.call-done = bf16[64,256,256]{2,1,0:T(8,128)(2,1)} async-done(((bf16[4,256,256]{2,1,0:T(8,128)(2,1)}), bf16[64,256,256]{2,1,0:T(8,128)(2,1)}) %all-gather.5.cloned.1.call-update) | async-done | bytes 8388624 | tf_op jit(solution)/shard_map/all_gather | solution.py:49
  153.8 0.0 all-gather.7.cloned.1.call-update
  153.8 34.5 %all-gather.7.cloned.1.call-done = bf16[16,8,256,256]{3,2,1,0:T(8,128)(2,1)} async-done(((bf16[16,4,256,256]{3,2,1,0:T(8,128)(2,1)}), bf16[16,8,256,256]{3,2,1,0:T(8,128)(2,1)}) %all-gather.7.cloned.1.call-update) | async-done | bytes 16777232 | tf_op jit(solution)/shard_map/all_gather | solution.py:50
  188.3 24.1 %fusion = bf16[1024,32,1,256]{3,0,1,2:T(8,128)(2,1)} fusion(bf16[32,4,256,256]{3,2,1,0:T(8,128)(2,1)} %bitcast.37, bf16[8,1024,256]{2,1,0:T(8,128)(2,1)} %copy-done.1, s32[]{:T(128)S(6)} %select_n.32), kind=kOutput, calls=%fused_computation.2 | convolution fusion | flops 17188257792 | bytes 35651588 | tf_op jit(solution)/shard_map/pmi,rpki->mrk/dot_general | solution.py:53
  212.4 17.9 %copy.8 = bf16[1024,32,1,256]{3,1,2,0:T(8,128)(2,1)} copy(bf16[1024,32,1,256]{3,0,1,2:T(8,128)(2,1)} %fusion) | data formatting | bytes 33554432 | tf_op jit(solution)/shard_map/reshape | solution.py:54
  (9 shorter events, 0.3 us)
Async XLA Ops:
  6.5 147.3 %all-gather.5.cloned.1.call-start = ((), (), s32[]{:S(2)}) async-start(), calls=%async_computation | async-start | bytes 8912896 | tf_op jit(solution)/shard_map/all_gather | solution.py:49
  6.5 13.6 %collective-permute-start = (bf16[1024,256]{1,0:T(8,128)(2,1)}, bf16[1024,256]{1,0:T(8,128)(2,1)S(1)}, u32[]{:S(2)}, u32[]{:S(2)}) collective-permute-start(bf16[1024,256]{1,0:T(8,128)(2,1)} %param.5), channel_id=1, source_target_pairs={{0,1},{1,2},{2,3},{3,4},{4,5},{5,6},{6,7},{7,8},{8,9},{9,10},{10,1... | collective-permute-start | bytes 1572872 | tf_op jit(solution)/shard_map/ppermute | solution.py:12
  11.1 10.7 %collective-permute-start.1 = (bf16[1024,256]{1,0:T(8,128)(2,1)}, bf16[1024,256]{1,0:T(8,128)(2,1)S(1)}, u32[]{:S(2)}, u32[]{:S(2)}) collective-permute-start(bf16[1024,256]{1,0:T(8,128)(2,1)} %param.5), channel_id=1, source_target_pairs={{1,0},{2,1},{3,2},{4,3},{5,4},{6,5},{7,6},{8,7},{9,8},{10,9},{11,1... | collective-permute-start | bytes 1572872 | tf_op jit(solution)/shard_map/ppermute | solution.py:15
  14.5 7.3 %copy-start = (bf16[1024,256]{1,0:T(8,128)(2,1)S(1)}, bf16[1024,256]{1,0:T(8,128)(2,1)}, u32[]{:S(2)}) copy-start(bf16[1024,256]{1,0:T(8,128)(2,1)} %param.5) | copy-start | bytes 1572868
  36.1 11.3 %collective-permute-start.2 = (bf16[1,1024,256]{2,1,0:T(8,128)(2,1)S(1)}, bf16[1,1024,256]{2,1,0:T(8,128)(2,1)S(1)}, u32[]{:S(2)}, u32[]{:S(2)}) collective-permute-start(bf16[1,1024,256]{2,1,0:T(8,128)(2,1)S(1)} %bitcast.34), channel_id=1, source_target_pairs={{0,32},{32,64},{64,96},{96,0},{1,33},{33,65},{65,97},{97,1},{2,34}... | collective-permute-start | bytes 1572872 | tf_op jit(solution)/shard_map/ppermute | solution.py:43
  47.3 12.3 %collective-permute-start.3 = (bf16[1,1024,256]{2,1,0:T(8,128)(2,1)S(1)}, bf16[1,1024,256]{2,1,0:T(8,128)(2,1)S(1)}, u32[]{:S(2)}, u32[]{:S(2)}) collective-permute-start(bf16[1,1024,256]{2,1,0:T(8,128)(2,1)S(1)} %collective-permute-done.2), channel_id=1, source_target_pairs={{0,32},{32,64},{64,96},{96,0},{1,33},{33,65},{65,97},{97,1},{2,34}... | collective-permute-start | bytes 1572872 | tf_op jit(solution)/shard_map/ppermute | solution.py:43
  59.6 13.4 %collective-permute-start.4 = (bf16[1,1024,256]{2,1,0:T(8,128)(2,1)S(1)}, bf16[1,1024,256]{2,1,0:T(8,128)(2,1)S(1)}, u32[]{:S(2)}, u32[]{:S(2)}) collective-permute-start(bf16[1,1024,256]{2,1,0:T(8,128)(2,1)S(1)} %collective-permute-done.3), channel_id=1, source_target_pairs={{0,32},{32,64},{64,96},{96,0},{1,33},{33,65},{65,97},{97,1},{2,34}... | collective-permute-start | bytes 1572872 | tf_op jit(solution)/shard_map/ppermute | solution.py:43
  73.4 2.0 copy-start.1
  76.3 112.0 %all-gather.7.cloned.1.call-start = ((), (), s32[]{:S(2)}) async-start(), calls=%async_computation.1 | async-start | bytes 25165824 | tf_op jit(solution)/shard_map/all_gather | solution.py:50
Sparse Core Ops, SparseCore 0:
  76.4 77.3 all-gather.4
  155.5 32.7 all-gather.6
